TPU v7x, 256 devices: a whole 4x4x8 slice. The times are simulated.
256 devices in a mesh: dp: 64 (over z, x, core), mp: 4 (over y).
Axes of the slice: x: 4, y: 4, z: 8, core: 2. Of those that a mesh axis runs over, the one named last changes fastest.
Arguments:
- embed_table: float32 [16, 32768, 256], P('mp', 'dp'), may hold values from -5 to 5
- accum: float32 [16, 32768], P('mp', 'dp'), may hold values from 0.1 to 3
- stale_grad: bfloat16 [16, 32768, 256], P('mp', 'dp'), may hold values from -6 to 6
- grad_owner: int32 [16, 32768, 1], P('mp', 'dp'), may hold values from 0 to 63; in each aligned block of 512 rows (0 to 511, 512 to 1023, ..., all dimensions but the last counted through in order) at most 16 rows name the same one
- grad_row: int32 [16, 32768], P('mp', 'dp'), may hold values from 0 to 511
- lookup_owner: int32 [16, 32768, 1], P('mp', 'dp'), may hold values from 0 to 63; in each aligned block of 512 rows (0 to 511, 512 to 1023, ..., all dimensions but the last counted through in order) at most 16 rows name the same one
- lookup_row: int32 [16, 32768], P('mp', 'dp'), may hold values from 0 to 511
- bag_len: int32 [16, 16384], P('mp', 'dp'), may hold values from 1 to 2
- label: int32 [16384], P('dp'), may hold values 0 or 1
- up_factor_weight: bfloat16 [2, 512, 4096], P(None, None, 'mp'), may hold values from -0.25 to 0.25
- v_weight: bfloat16 [2, 512, 4096], P(None, None, 'mp'), may hold values from -0.09375 to 0.09375
- cross_bias: float32 [2, 4096], P(None, 'mp'), may hold values from -3 to 3
- head_weight: float32 [4096], P('mp'), may hold values from -0.09375 to 0.09375
Outputs:
- new_table: float32 [16, 32768, 256], P('mp', 'dp')
- new_accum: float32 [16, 32768], P('mp', 'dp')
- grad_u: float32 [2, 512, 4096], P(None, 'dp', 'mp')
- grad_v: float32 [2, 512, 4096], P(None, 'dp', 'mp')
- grad_small: float32 [3, 4096], P(None, 'mp')
- grad_pooled: bfloat16 [16384, 4096], P('dp', 'mp')
Inputs may be any that keep to these rules, and one draw needn't show every extreme that they name: `grad_owner`: among the 512 blocks of one feature held by one index of dp, at most 16 name the same owner, and in some such group exactly 16 do. `lookup_owner`: among the 512 id slots of one feature belonging to one index of dp, at most 16 name the same owner, and in some such group exactly 16 do; slots k >= bag_len are unused.
All inputs are finite; a program needn't handle non-finite values. No bound on the sum of `label` on one device may be relied on, other than what follows from the above.
Results may differ from a plain program's by a relative error of at most 0.009.
Values may be sent and summed in bfloat16 or wider, within the bound.
No kernel may reach another device: no remote copies, remote signals or barrier semaphores. Data moves between devices by JAX's collectives and lax.ppermute only.
A program may use at most 128 MiB of HBM per device.

v0:
```python
import jax
import jax.numpy as jnp
from jax import lax
from jax.sharding import PartitionSpec as P

learn_rate = 0.5


def in_blocks(array, dim, devices):
    shape = array.shape
    parts = array.reshape(*shape[:dim], devices, shape[dim] // devices, *shape[dim + 1 :])
    return jnp.moveaxis(parts, dim, 0)


def sum_at_owner(array, axis, dim):
    parts = in_blocks(array, dim, lax.axis_size(axis))
    arrived = lax.all_to_all(parts, axis, split_axis=0, concat_axis=0, tiled=True)
    return arrived.sum(axis=0)


def copy_for_each(array, axis):
    copies = jnp.broadcast_to(array, (lax.axis_size(axis), *array.shape))
    return lax.all_to_all(copies, axis, split_axis=0, concat_axis=0, tiled=True)


def over_copies(array, axis):
    return copy_for_each(array, axis).sum(axis=0)


def side_by_side(arrays, axis, dim, along):
    widths = [a.shape[along] for a in arrays]
    both = jnp.concatenate(arrays, axis=along)
    filled = lax.psum_scatter(both, axis, scatter_dimension=dim, tiled=True)
    return tuple(jnp.split(filled, [sum(widths[:k]) for k in range(1, len(widths))], axis=along))


def bucket_slots(owners, capacity, peers):
    count = owners.shape[1]
    onehot = (owners[:, None, :] == jnp.arange(peers)[None, :, None]).astype(jnp.bfloat16)
    earlier = (jnp.arange(count)[:, None] < jnp.arange(count)[None, :]).astype(jnp.bfloat16)
    before = jnp.einsum("fpi,ij->fpj", onehot, earlier, preferred_element_type=jnp.float32)
    order_in = jnp.sum(before * onehot.astype(jnp.float32), axis=1)
    return owners * capacity + order_in.astype(jnp.int32)


def selection_matrix(indices, length):
    return (indices[:, :, None] == jnp.arange(length)[None, None, :]).astype(jnp.bfloat16)


def contract_last(left, right):
    return lax.dot_general(
        left, right, (((1,), (1,)), ((), ())), preferred_element_type=jnp.float32
    )


def contract_first(left, right):
    return lax.dot_general(
        left, right, (((0,), (0,)), ((), ())), preferred_element_type=jnp.float32
    )


def summed_rounded(partial, axis):
    share = lax.psum_scatter(partial, axis, scatter_dimension=0, tiled=True)
    return lax.all_gather(share.astype(jnp.bfloat16), axis, axis=0, tiled=True)


def cross_down(state, v_layer):
    return summed_rounded(contract_last(state, v_layer), "mp")


def local(
    embed_table,
    accum,
    stale_grad,
    grad_owner,
    grad_row,
    lookup_owner,
    lookup_row,
    bag_len,
    label,
    up_factor_weight,
    v_weight,
    cross_bias,
    head_weight,
):
    peers = lax.axis_size("dp")
    local_feats, grad_dev, width = stale_grad.shape
    rows_per_shard = embed_table.shape[1]
    which_feature = jnp.arange(local_feats)[:, None]
    grad_cap = max(2, 2 * grad_dev // peers)
    grad_total = peers * grad_cap
    grad_slot = bucket_slots(grad_owner[:, :, 0], grad_cap, peers)
    place = selection_matrix(grad_slot, grad_total)
    send_grads = jnp.einsum(
        "fns,fne->fse", place, stale_grad, preferred_element_type=jnp.float32
    ).astype(jnp.bfloat16)
    send_rows = (
        jnp.full((local_feats, grad_total), rows_per_shard, jnp.int32)
        .at[which_feature, grad_slot]
        .set(grad_row)
    )
    recv_grads = lax.all_to_all(
        send_grads.reshape(local_feats, peers, grad_cap, width),
        "dp",
        split_axis=1,
        concat_axis=1,
        tiled=True,
    )
    recv_rows = lax.all_to_all(
        send_rows.reshape(local_feats, peers, grad_cap),
        "dp",
        split_axis=1,
        concat_axis=1,
        tiled=True,
    )
    landing = selection_matrix(recv_rows.reshape(local_feats, grad_total), rows_per_shard)
    summed = jnp.einsum(
        "wjc,wjl->wcl",
        landing,
        recv_grads.reshape(local_feats, grad_total, width),
        preferred_element_type=jnp.float32,
    )
    new_accum = accum + jnp.mean(summed * summed, axis=2)
    new_table = embed_table - learn_rate * summed / jnp.sqrt(new_accum)[:, :, None]
    batch_dev = bag_len.shape[1]
    look_dev = lookup_row.shape[1]
    bag_size = look_dev // batch_dev
    look_cap = max(2, 2 * look_dev // peers)
    look_total = peers * look_cap
    look_slot = bucket_slots(lookup_owner[:, :, 0], look_cap, peers)
    wanted = (
        jnp.zeros((local_feats, look_total), jnp.int32).at[which_feature, look_slot].set(lookup_row)
    )
    requested_ids = lax.all_to_all(
        wanted.reshape(local_feats, peers, look_cap), "dp", split_axis=1, concat_axis=1, tiled=True
    ).reshape(local_feats, look_total)
    second_table = embed_table.astype(jnp.bfloat16)
    served = jnp.einsum(
        "adv,avm->adm",
        selection_matrix(requested_ids, rows_per_shard),
        second_table,
        preferred_element_type=jnp.float32,
    ).astype(jnp.bfloat16)
    returned = lax.all_to_all(
        served.reshape(local_feats, peers, look_cap, width),
        "dp",
        split_axis=1,
        concat_axis=1,
        tiled=True,
    ).reshape(local_feats, look_total, width)
    slots = look_slot.reshape(local_feats, batch_dev, bag_size)
    mixing = jnp.zeros((local_feats, batch_dev, look_total), jnp.bfloat16)
    for member in range(bag_size):
        used = (bag_len > member).astype(jnp.bfloat16)
        mixing = mixing + selection_matrix(slots[:, :, member], look_total) * used[:, :, None]
    pooled = jnp.einsum(
        "fbs,fse->fbe", mixing, returned, preferred_element_type=jnp.float32
    ).astype(jnp.bfloat16)
    start = jnp.transpose(pooled, (1, 0, 2)).reshape(batch_dev, local_feats * width)
    start_f = start.astype(jnp.float32)
    n_layers = up_factor_weight.shape[0]
    state = start
    states = []
    downs = []
    crosses = []
    for layer in range(n_layers):
        down_sum = cross_down(state, v_weight[layer])
        cross_out = (
            jnp.dot(down_sum, up_factor_weight[layer], preferred_element_type=jnp.float32)
            + cross_bias[layer]
        )
        states.append(state)
        downs.append(down_sum)
        crosses.append(cross_out)
        state = (start_f * cross_out + state.astype(jnp.float32)).astype(jnp.bfloat16)
    logit = lax.psum(jnp.sum(state.astype(jnp.float32) * head_weight[None, :], axis=1), "mp")
    slope = (jax.nn.sigmoid(logit) - label.astype(jnp.float32)) / jnp.sqrt(
        jnp.float32(batch_dev * peers)
    )
    upstream = slope[:, None] * head_weight[None, :]
    head_grad = jnp.sum(slope[:, None] * state.astype(jnp.float32), axis=0)
    to_start = jnp.zeros(start_f.shape, jnp.float32)
    grads_u = [None] * n_layers
    grads_v = [None] * n_layers
    bias_grads = [None] * n_layers
    for layer in reversed(range(n_layers)):
        direct = upstream * start_f
        bias_grads[layer] = jnp.sum(direct, axis=0)
        direct_bias_term = direct.astype(jnp.bfloat16)
        grad_u_layer = contract_first(downs[layer], direct_bias_term)
        back_sum = summed_rounded(contract_last(direct_bias_term, up_factor_weight[layer]), "mp")
        down_factor_gradient = contract_first(back_sum, states[layer])
        to_start = to_start + upstream * crosses[layer]
        upstream = upstream + jnp.dot(back_sum, v_weight[layer], preferred_element_type=jnp.float32)
        grads_u[layer] = grad_u_layer
        grads_v[layer] = down_factor_gradient
    grad_u = jnp.stack(grads_u)
    grad_v = jnp.stack(grads_v)
    grad_u, grad_v = side_by_side((grad_u, grad_v), "dp", 1, 0)
    grad_small = lax.psum(jnp.stack(bias_grads + [head_grad]), "dp")
    grad_pooled = (upstream + to_start).astype(jnp.bfloat16)
    return (new_table, new_accum, grad_u, grad_v, grad_small, grad_pooled)


def solution(mesh):
    return jax.shard_map(
        local,
        mesh=mesh,
        in_specs=(
            P("mp", "dp", None),
            P("mp", "dp"),
            P("mp", "dp", None),
            P("mp", "dp", None),
            P("mp", "dp"),
            P("mp", "dp", None),
            P("mp", "dp"),
            P("mp", "dp"),
            P("dp"),
            P(None, None, "mp"),
            P(None, None, "mp"),
            P(None, "mp"),
            P("mp"),
        ),
        out_specs=(
            P("mp", "dp", None),
            P("mp", "dp"),
            P(None, "dp", "mp"),
            P(None, "dp", "mp"),
            P(None, "mp"),
            P("dp", "mp"),
        ),
        check_vma=False,
    )
```

profile of v0, /device:TPU:0, one launch (start us, length us, event | category | flops | bytes accessed | tf_op | source)
XLA Modules:
  0.0 633.7 jit_solution(6955148603846393421)
XLA Ops:
  10.6 8.1 %scatter_custom_fusion.1 = s32[4096]{0:T(1024)S(1)} fusion(s32[2048]{0:T(1024)S(1)} %bitcast.111, s32[2048]{0:T(1024)S(1)} %bitcast.113, s32[]{:T(128)} %constant.5.clone.1), kind=kCustom, calls=%fused_computation.105 | custom fusion | bytes 16388
  18.9 21.1 %all_to_all.20 = s32[4,64,16]{2,0,1:T(4,128)S(1)} all-to-all(s32[4,64,16]{2,0,1:T(4,128)S(1)} %copy.43), channel_id=1, replica_groups=mesh['dp'=64,'mp'=4] {'dp'}, dimensions={1} | all-to-all | bytes 32768 | tf_op jit(solution)/shard_map/all_to_all | solution.py:134
  40.1 2.1 fusion.14
  42.1 1.6 copy.45
  43.8 4.7 all-to-all-start.3
  49.6 1.1 add.86
  51.0 48.8 %all-to-all-done.3 = bf16[4,64,16,256]{3,2,0,1:T(8,128)(2,1)S(1)} async-done(((bf16[4,64,16,256]{3,2,0,1:T(8,128)(2,1)}), bf16[4,64,16,256]{3,2,0,1:T(8,128)(2,1)S(1)}, u32[]{:S(2)}, u32[]{:S(2)}) %all-to-all-start.3) | async-done | bytes 2097184 | tf_op jit(solution)/shard_map/all_to_all | solution.py:144
  100.0 2.1 fusion.17
  102.1 1.3 fusion.40
  103.7 20.2 %reduce-scatter.6.cloned.1.call-done = f32[64,512]{1,0:T(8,128)} async-done(((f32[256,512]{1,0:T(8,128)}), f32[64,512]{1,0:T(8,128)}) %reduce-scatter.6.cloned.1.call-update) | async-done | bytes 131088 | tf_op jit(solution)/shard_map/reduce_scatter | solution.py:63
  123.9 1.1 convert_element_type.138
  125.0 12.3 %all_gather.12 = bf16[256,512]{1,0:T(8,128)(2,1)S(1)} all-gather(bf16[64,512]{1,0:T(8,128)(2,1)S(1)} %convert_element_type.138), channel_id=1, replica_groups=mesh['dp'=64,'mp'=4] {'mp'}, dimensions={0}, use_global_device_ids=true | all-gather | bytes 327680 | tf_op jit(solution)/shard_map/all_gather | solution.py:64
  137.3 2.8 fusion.26
  140.1 1.3 fusion.34
  141.5 23.9 %reduce-scatter.8.cloned.1.call-done = f32[64,512]{1,0:T(8,128)} async-done(((f32[256,512]{1,0:T(8,128)}), f32[64,512]{1,0:T(8,128)}) %reduce-scatter.8.cloned.1.call-update) | async-done | bytes 131088 | tf_op jit(solution)/shard_map/reduce_scatter | solution.py:63
  165.3 0.9 convert_element_type.141
  166.3 12.3 %all_gather.13 = bf16[256,512]{1,0:T(8,128)(2,1)S(1)} all-gather(bf16[64,512]{1,0:T(8,128)(2,1)S(1)} %convert_element_type.141), channel_id=1, replica_groups=mesh['dp'=64,'mp'=4] {'mp'}, dimensions={0}, use_global_device_ids=true | all-gather | bytes 327680 | tf_op jit(solution)/shard_map/all_gather | solution.py:64
  178.5 2.9 fusion.23
  181.4 8.4 %psum.14 = f32[256]{0:T(256)S(1)} all-reduce(f32[256]{0:T(256)S(1)} %get-tuple-element.28), channel_id=1, replica_groups=mesh['dp'=64,'mp'=4] {'mp'}, use_global_device_ids=true, to_apply=%region_8.0 | all-reduce | flops 256 | bytes 2048 | tf_op jit(solution)/shard_map/psum | solution.py:176
  190.2 2.5 fusion.30
  192.8 23.7 %reduce-scatter.10.cloned.1.call-done = f32[64,512]{1,0:T(8,128)} async-done(((f32[256,512]{1,0:T(8,128)}), f32[64,512]{1,0:T(8,128)}) %reduce-scatter.10.cloned.1.call-update) | async-done | bytes 131088 | tf_op jit(solution)/shard_map/reduce_scatter | solution.py:63
  216.5 1.1 convert_element_type.149
  217.5 12.3 %all_gather.14 = bf16[256,512]{1,0:T(8,128)(2,1)S(1)} all-gather(bf16[64,512]{1,0:T(8,128)(2,1)S(1)} %convert_element_type.149), channel_id=1, replica_groups=mesh['dp'=64,'mp'=4] {'mp'}, dimensions={0}, use_global_device_ids=true | all-gather | bytes 327680 | tf_op jit(solution)/shard_map/all_gather | solution.py:64
  230.5 1.7 fusion.59
  232.2 1.3 fusion.36
  233.8 1.9 convolution_bitcast_fusion.2
  235.7 1.8 convolution_bitcast_fusion
  237.5 1.8 convolution_bitcast_fusion.3
  239.3 18.1 %reduce-scatter.12.cloned.1.call-done = f32[64,512]{1,0:T(8,128)} async-done(((f32[256,512]{1,0:T(8,128)}), f32[64,512]{1,0:T(8,128)}) %reduce-scatter.12.cloned.1.call-update) | async-done | bytes 131088 | tf_op jit(solution)/shard_map/reduce_scatter | solution.py:63
  257.4 1.1 convert_element_type.152
  258.5 12.3 %all_gather.15 = bf16[256,512]{1,0:T(8,128)(2,1)S(1)} all-gather(bf16[64,512]{1,0:T(8,128)(2,1)S(1)} %convert_element_type.152), channel_id=1, replica_groups=mesh['dp'=64,'mp'=4] {'mp'}, dimensions={0}, use_global_device_ids=true | all-gather | bytes 327680 | tf_op jit(solution)/shard_map/all_gather | solution.py:64
  271.2 5.2 pad_maximum_fusion
  277.1 8.1 %scatter_custom_fusion = s32[4096]{0:T(1024)S(1)} fusion(s32[2048]{0:T(1024)S(1)} %bitcast.112, s32[2048]{0:T(1024)S(1)} %bitcast.114, s32[]{:T(128)} %constant.11.clone.1), kind=kCustom, calls=%fused_computation.107 | custom fusion | bytes 16388
  286.0 10.4 %all-to-all-start = ((s32[4,64,16]{2,0,1:T(4,128)}), s32[4,64,16]{2,0,1:T(4,128)S(1)}, u32[]{:S(2)}, u32[]{:S(2)}) async-start(s32[4,64,16]{2,0,1:T(4,128)} %copy.33), calls=%async_computation | async-start | bytes 262144 | tf_op jit(solution)/shard_map/all_to_all | solution.py:109
  296.5 1.5 fusion.15
  298.0 1.6 copy.35
  299.6 7.9 %all-to-all-done = s32[4,64,16]{2,0,1:T(4,128)S(1)} async-done(((s32[4,64,16]{2,0,1:T(4,128)}), s32[4,64,16]{2,0,1:T(4,128)S(1)}, u32[]{:S(2)}, u32[]{:S(2)}) %all-to-all-start) | async-done | bytes 16416 | tf_op jit(solution)/shard_map/all_to_all | solution.py:109
  307.5 5.6 all-to-all-start.1
  313.1 2.9 copy.38
  316.2 49.0 %all-to-all-done.1 = bf16[4,64,16,256]{3,2,0,1:T(8,128)(2,1)} async-done(((bf16[4,64,16,256]{3,2,0,1:T(8,128)(2,1)}), bf16[4,64,16,256]{3,2,0,1:T(8,128)(2,1)}, u32[]{:S(2)}, u32[]{:S(2)}) %all-to-all-start.1) | async-done | bytes 2097184 | tf_op jit(solution)/shard_map/all_to_all | solution.py:102
  365.1 1.8 copy.36
  367.0 2.9 multiply_reduce_fusion
  370.5 1.9 divide_subtract_fusion
  372.4 3.0 copy.49
  375.4 1.2 fusion.24
  376.6 246.2 %psum.15 = f32[3,1024]{1,0:T(4,128)} all-reduce(f32[3,1024]{1,0:T(4,128)S(1)} %pad_maximum_fusion.1), channel_id=1, replica_groups=mesh['dp'=64,'mp'=4] {'dp'}, use_global_device_ids=true, to_apply=%region_15.0 | all-reduce | flops 3072 | bytes 24576 | tf_op jit(solution)/shard_map/psum | solution.py:200
  622.8 2.8 fusion.20
  625.6 1.5 fusion.79
  (100 shorter events, 9.8 us)
Async XLA Ops:
  7.2 289.3 %copy-start = (bf16[4,512,256]{2,1,0:T(8,128)(2,1)S(1)}, bf16[4,512,256]{2,1,0:T(8,128)(2,1)}, u32[]{:S(2)}) copy-start(bf16[4,512,256]{2,1,0:T(8,128)(2,1)} %param.15) | copy-start | bytes 3145732
  7.2 3.1 copy-start.23
  7.2 3.2 copy-start.22
  7.2 3.0 copy-start.15
  7.2 3.4 copy-start.16
  7.2 32.8 %copy-start.9 = (f32[4,512,256]{2,1,0:T(8,128)S(1)}, f32[4,512,256]{2,1,0:T(8,128)}, u32[]{:S(2)}) copy-start(f32[4,512,256]{2,1,0:T(8,128)} %param.13) | copy-start | bytes 6291460
  43.8 56.1 %all-to-all-start.3 = ((bf16[4,64,16,256]{3,2,0,1:T(8,128)(2,1)}), bf16[4,64,16,256]{3,2,0,1:T(8,128)(2,1)S(1)}, u32[]{:S(2)}, u32[]{:S(2)}) async-start(bf16[4,64,16,256]{3,2,0,1:T(8,128)(2,1)} %copy.45), calls=%async_computation.3 | async-start | bytes 4194304 | tf_op jit(solution)/shard_map/all_to_all | solution.py:144
  48.5 2.5 copy-start.20
  48.5 75.4 %reduce-scatter.6.cloned.1.call-start = ((), (), s32[]{:S(2)}) async-start(), calls=%async_computation.9 | async-start | bytes 655360 | tf_op jit(solution)/shard_map/reduce_scatter | solution.py:63
  100.0 2.1 copy-start.12
  102.1 1.4 copy-start.17
  103.4 61.9 %reduce-scatter.8.cloned.1.call-start = ((), (), s32[]{:S(2)}) async-start(), calls=%async_computation.10 | async-start | bytes 655360 | tf_op jit(solution)/shard_map/reduce_scatter | solution.py:63
  123.9 16.2 %copy-start.13 = (bf16[2,512,1024]{2,1,0:T(8,128)(2,1)S(1)}, bf16[2,512,1024]{2,1,0:T(8,128)(2,1)}, u32[]{:S(2)}) copy-start(bf16[2,512,1024]{2,1,0:T(8,128)(2,1)} %param.23) | copy-start | bytes 6291460
  137.3 4.1 copy-start.7
  140.1 41.3 %copy-start.4 = (bf16[256,1024]{1,0:T(8,128)(2,1)}, bf16[256,1024]{1,0:T(8,128)(2,1)S(1)}, u32[]{:S(2)}) copy-start(bf16[256,1024]{1,0:T(8,128)(2,1)S(1)} %get-tuple-element.48) | copy-start | bytes 1572868
  140.1 1.4 copy-start.14
  141.4 75.1 %reduce-scatter.10.cloned.1.call-start = ((), (), s32[]{:S(2)}) async-start(), calls=%async_computation.11 | async-start | bytes 655360 | tf_op jit(solution)/shard_map/reduce_scatter | solution.py:63
  166.2 23.5 %copy-start.21 = (s32[256]{0:T(256)S(1)}, s32[256]{0:T(256)}, u32[]{:S(2)}) copy-start(s32[256]{0:T(256)} %param.21) | copy-start | bytes 3076
  192.7 64.7 %reduce-scatter.12.cloned.1.call-start = ((), (), s32[]{:S(2)}) async-start(), calls=%async_computation.12 | async-start | bytes 655360 | tf_op jit(solution)/shard_map/reduce_scatter | solution.py:63
  216.5 15.7 %copy-start.3 = (bf16[2,512,1024]{2,1,0:T(8,128)(2,1)S(1)}, bf16[2,512,1024]{2,1,0:T(8,128)(2,1)}, u32[]{:S(2)}) copy-start(bf16[2,512,1024]{2,1,0:T(8,128)(2,1)} %param.22) | copy-start | bytes 6291460
  229.8 0.7 copy-start.10
  233.5 392.1 %reduce-scatter.14.cloned.1.call-start = ((), (), s32[]{:S(2)}) async-start(), calls=%async_computation.13 | async-start | bytes 8519680 | tf_op jit(solution)/shard_map/reduce_scatter | solution.py:33
  233.8 1.9 copy-start.5
  233.8 1.9 copy-start.11
  235.7 1.8 copy-start.8
  257.4 13.8 %copy-start.2 = (f32[1,512,1024]{2,1,0:T(8,128)S(1)}, f32[1,512,1024]{2,1,0:T(8,128)}, u32[]{:S(2)}) copy-start(f32[1,512,1024]{2,1,0:T(8,128)} %convolution_bitcast_fusion.2) | copy-start | bytes 6291460
  276.4 0.7 copy-start.18
  286.0 21.5 %all-to-all-start = ((s32[4,64,16]{2,0,1:T(4,128)}), s32[4,64,16]{2,0,1:T(4,128)S(1)}, u32[]{:S(2)}, u32[]{:S(2)}) async-start(s32[4,64,16]{2,0,1:T(4,128)} %copy.33), calls=%async_computation | async-start | bytes 262144 | tf_op jit(solution)/shard_map/all_to_all | solution.py:109
  307.5 57.6 %all-to-all-start.1 = ((bf16[4,64,16,256]{3,2,0,1:T(8,128)(2,1)}), bf16[4,64,16,256]{3,2,0,1:T(8,128)(2,1)}, u32[]{:S(2)}, u32[]{:S(2)}) async-start(bf16[4,64,16,256]{3,2,0,1:T(8,128)(2,1)} %copy.35), calls=%async_computation.1 | async-start | bytes 4194304 | tf_op jit(solution)/shard_map/all_to_all | solution.py:102
  366.9 2.9 copy-start.19
  367.0 3.5 copy-start.1
  372.4 250.5 %copy-start.6 = (f32[256,1024]{1,0:T(8,128)S(1)}, f32[256,1024]{1,0:T(8,128)}, u32[]{:S(2)}) copy-start(f32[256,1024]{1,0:T(8,128)} %get-tuple-element.50) | copy-start | bytes 3145732
Sparse Core Ops, SparseCore 0:
  103.5 20.3 reduce-scatter.5
  141.5 23.7 reduce-scatter.7
  192.8 23.5 reduce-scatter.9
  233.7 23.7 reduce-scatter.11
  276.6 150.7 reduce-scatter.13
where the time goes:
time: 635 us; the launch traced here: 634 us
  blocking collectives  325 us (51%)
  waiting for transfers between devices  192 us (30%)
  local copies, waits for them, and re-layouts  34.7 us (5%)
  matrix products  31.7 us (5%)
  starting transfers between devices  21.1 us (3%)
  other arithmetic  15.5 us (2%)
  between operations  14.3 us (2%)
    psum x1, blocking collectives, local(): grad_small = lax.psum(jnp.stack(bias_grads + [head_grad]), 'dp')  246 us
    reduce_scatter x4, waiting for transfers between devices, summed_rounded(): share = lax.psum_scatter(partial, axis, scatter_dimension=0, tiled=True)  85.9 us
    all_gather x4, blocking collectives, summed_rounded(): return lax.all_gather(share.astype(jnp.bfloat16), axis, axis=0, tiled=True)  49 us
    all_to_all x1, waiting for transfers between devices, local(): lax.all_to_all(send_grads.reshape(local_feats, peers, grad_cap, width), '...  49 us
    all_to_all x1, waiting for transfers between devices, local(): lax.all_to_all(served.reshape(local_feats, peers, look_cap, width), 'dp',...  48.8 us
    unnamed x60, local copies, waits for them, and re-layouts  25.1 us
    all_to_all x1, blocking collectives, local(): lax.all_to_all(wanted.reshape(local_feats, peers, look_cap), 'dp', split_...  21.1 us
  transfers between devices with their start and end apart: 8, of which 7 were waited for; matrix products, arithmetic and copies ran while one was open for 6% of the time, Pallas kernels for 0%

commit v1 on v0

--- a/solution.py
+++ b/solution.py
@@ -197,7 +197,7 @@
     grad_u = jnp.stack(grads_u)
     grad_v = jnp.stack(grads_v)
     grad_u, grad_v = side_by_side((grad_u, grad_v), "dp", 1, 0)
-    grad_small = lax.psum(jnp.stack(bias_grads + [head_grad]), "dp")
+    grad_small = jnp.sum(lax.all_gather(jnp.stack(bias_grads + [head_grad]), "dp"), axis=0)
     grad_pooled = (upstream + to_start).astype(jnp.bfloat16)
     return (new_table, new_accum, grad_u, grad_v, grad_small, grad_pooled)
 

time: 635 us -> 448 us (0.71)
  blocking collectives: 325 us -> 133 us
    psum x1 -> x0, blocking collectives: 246 us -> none  [local(): grad_small = lax.psum(jnp.stack(bias_grads + [head_grad]), 'dp')]
    all_gather x0 -> x1, blocking collectives: none -> 54.5 us  [local(): lax.all_gather(jnp.stack(bias_grads + [head_grad]), 'dp')]
  transfers between devices with their start and end apart: 8 -> 8, of which waited for: 7 -> 7; matrix products, arithmetic and copies ran while one was open for 6% -> 9% of each run, Pallas kernels for 0% -> 0%
where the time goes in v1:
time: 448 us; the launch traced here: 444 us
  waiting for transfers between devices  192 us (43%)
  blocking collectives  133 us (30%)
  local copies, waits for them, and re-layouts  34.6 us (8%)
  matrix products  31.7 us (7%)
  starting transfers between devices  21.1 us (5%)
  other arithmetic  17.6 us (4%)
  between operations  14.3 us (3%)
    reduce_scatter x4, waiting for transfers between devices, summed_rounded(): share = lax.psum_scatter(partial, axis, scatter_dimension=0, tiled=True)  85.9 us
    all_gather x1, blocking collectives, local(): lax.all_gather(jnp.stack(bias_grads + [head_grad]), 'dp')  54.5 us
    all_gather x4, blocking collectives, summed_rounded(): return lax.all_gather(share.astype(jnp.bfloat16), axis, axis=0, tiled=True)  49 us
    all_to_all x1, waiting for transfers between devices, local(): lax.all_to_all(send_grads.reshape(local_feats, peers, grad_cap, width), '...  49 us
    all_to_all x1, waiting for transfers between devices, local(): lax.all_to_all(served.reshape(local_feats, peers, look_cap, width), 'dp',...  48.8 us
    unnamed x60, local copies, waits for them, and re-layouts  25 us
    all_to_all x1, blocking collectives, local(): lax.all_to_all(wanted.reshape(local_feats, peers, look_cap), 'dp', split_...  21.1 us
    all_to_all x1, starting transfers between devices, local(): lax.all_to_all(send_rows.reshape(local_feats, peers, grad_cap), 'dp', spl...  10.4 us
  transfers between devices with their start and end apart: 8, of which 7 were waited for; matrix products, arithmetic and copies ran while one was open for 9% of the time, Pallas kernels for 0%

profile of v1, /device:TPU:0, one launch (start us, length us, event | category | flops | bytes accessed | tf_op | source)
XLA Modules:
  0.0 444.1 jit_solution(10069818290897851126)
XLA Ops:
  10.6 8.1 %scatter_custom_fusion.1 = s32[4096]{0:T(1024)S(1)} fusion(s32[2048]{0:T(1024)S(1)} %bitcast.113, s32[2048]{0:T(1024)S(1)} %bitcast.115, s32[]{:T(128)} %constant.5.clone.1), kind=kCustom, calls=%fused_computation.105 | custom fusion | bytes 16388
  18.9 21.1 %all_to_all.20 = s32[4,64,16]{2,0,1:T(4,128)S(1)} all-to-all(s32[4,64,16]{2,0,1:T(4,128)S(1)} %copy.43), channel_id=1, replica_groups=mesh['dp'=64,'mp'=4] {'dp'}, dimensions={1} | all-to-all | bytes 32768 | tf_op jit(solution)/shard_map/all_to_all | solution.py:134
  40.1 2.1 fusion.14
  42.1 1.6 copy.45
  43.8 4.7 %all-to-all-start.3 = ((bf16[4,64,16,256]{3,2,0,1:T(8,128)(2,1)}), bf16[4,64,16,256]{3,2,0,1:T(8,128)(2,1)S(1)}, u32[]{:S(2)}, u32[]{:S(2)}) async-start(bf16[4,64,16,256]{3,2,0,1:T(8,128)(2,1)} %copy.45), calls=%async_computation.3 | async-start | bytes 4194304 | tf_op jit(solution)/shard_map/all_to_all | solution.py:144
  49.6 1.1 add.84
  51.0 48.8 %all-to-all-done.3 = bf16[4,64,16,256]{3,2,0,1:T(8,128)(2,1)S(1)} async-done(((bf16[4,64,16,256]{3,2,0,1:T(8,128)(2,1)}), bf16[4,64,16,256]{3,2,0,1:T(8,128)(2,1)S(1)}, u32[]{:S(2)}, u32[]{:S(2)}) %all-to-all-start.3) | async-done | bytes 2097184 | tf_op jit(solution)/shard_map/all_to_all | solution.py:144
  100.0 2.1 fusion.17
  102.1 1.3 fusion.40
  103.7 20.2 %reduce-scatter.6.cloned.1.call-done = f32[64,512]{1,0:T(8,128)} async-done(((f32[256,512]{1,0:T(8,128)}), f32[64,512]{1,0:T(8,128)}) %reduce-scatter.6.cloned.1.call-update) | async-done | bytes 131088 | tf_op jit(solution)/shard_map/reduce_scatter | solution.py:63
  123.9 1.1 convert_element_type.138
  125.0 12.3 %all_gather.18 = bf16[256,512]{1,0:T(8,128)(2,1)S(1)} all-gather(bf16[64,512]{1,0:T(8,128)(2,1)S(1)} %convert_element_type.138), channel_id=1, replica_groups=mesh['dp'=64,'mp'=4] {'mp'}, dimensions={0}, use_global_device_ids=true | all-gather | bytes 327680 | tf_op jit(solution)/shard_map/all_gather | solution.py:64
  137.3 2.8 fusion.26
  140.1 1.3 fusion.34
  141.5 23.9 %reduce-scatter.8.cloned.1.call-done = f32[64,512]{1,0:T(8,128)} async-done(((f32[256,512]{1,0:T(8,128)}), f32[64,512]{1,0:T(8,128)}) %reduce-scatter.8.cloned.1.call-update) | async-done | bytes 131088 | tf_op jit(solution)/shard_map/reduce_scatter | solution.py:63
  166.3 12.3 %all_gather.19 = bf16[256,512]{1,0:T(8,128)(2,1)S(1)} all-gather(bf16[64,512]{1,0:T(8,128)(2,1)S(1)} %convert_element_type.141), channel_id=1, replica_groups=mesh['dp'=64,'mp'=4] {'mp'}, dimensions={0}, use_global_device_ids=true | all-gather | bytes 327680 | tf_op jit(solution)/shard_map/all_gather | solution.py:64
  178.5 2.9 fusion.23
  181.4 8.4 %psum.7 = f32[256]{0:T(256)S(1)} all-reduce(f32[256]{0:T(256)S(1)} %get-tuple-element.28), channel_id=1, replica_groups=mesh['dp'=64,'mp'=4] {'mp'}, use_global_device_ids=true, to_apply=%region_8.0 | all-reduce | flops 256 | bytes 2048 | tf_op jit(solution)/shard_map/psum | solution.py:176
  190.2 2.5 fusion.30
  192.8 23.7 %reduce-scatter.10.cloned.1.call-done = f32[64,512]{1,0:T(8,128)} async-done(((f32[256,512]{1,0:T(8,128)}), f32[64,512]{1,0:T(8,128)}) %reduce-scatter.10.cloned.1.call-update) | async-done | bytes 131088 | tf_op jit(solution)/shard_map/reduce_scatter | solution.py:63
  216.5 1.1 convert_element_type.149
  217.5 12.3 %all_gather.20 = bf16[256,512]{1,0:T(8,128)(2,1)S(1)} all-gather(bf16[64,512]{1,0:T(8,128)(2,1)S(1)} %convert_element_type.149), channel_id=1, replica_groups=mesh['dp'=64,'mp'=4] {'mp'}, dimensions={0}, use_global_device_ids=true | all-gather | bytes 327680 | tf_op jit(solution)/shard_map/all_gather | solution.py:64
  230.5 1.7 fusion.59
  232.2 1.3 fusion.36
  233.8 1.9 convolution_bitcast_fusion.2
  235.7 1.8 convolution_bitcast_fusion
  237.5 1.8 convolution_bitcast_fusion.3
  239.3 18.1 %reduce-scatter.12.cloned.1.call-done = f32[64,512]{1,0:T(8,128)} async-done(((f32[256,512]{1,0:T(8,128)}), f32[64,512]{1,0:T(8,128)}) %reduce-scatter.12.cloned.1.call-update) | async-done | bytes 131088 | tf_op jit(solution)/shard_map/reduce_scatter | solution.py:63
  257.4 1.1 convert_element_type.152
  258.5 12.3 %all_gather.21 = bf16[256,512]{1,0:T(8,128)(2,1)S(1)} all-gather(bf16[64,512]{1,0:T(8,128)(2,1)S(1)} %convert_element_type.152), channel_id=1, replica_groups=mesh['dp'=64,'mp'=4] {'mp'}, dimensions={0}, use_global_device_ids=true | all-gather | bytes 327680 | tf_op jit(solution)/shard_map/all_gather | solution.py:64
  271.3 5.2 %pad_maximum_fusion = f32[4,512,1024]{2,1,0:T(8,128)} fusion(f32[1,512,1024]{2,1,0:T(8,128)} %convolution_bitcast_fusion, f32[1,512,1024]{2,1,0:T(8,128)S(1)} %convolution_bitcast_fusion.1, f32[1,512,1024]{2,1,0:T(8,128)S(1)} %copy-done.2, f32[1,512,1024]{2,1,0:T(8,128)} %convolution_bitcast_fusion.3), kind=kLoop, calls=%fused_computation.2 | loop fusion | flops 6291456 | bytes 16777216 | tf_op jit(solution)/shard_map/concatenate | solution.py:32
  277.2 8.1 %scatter_custom_fusion = s32[4096]{0:T(1024)S(1)} fusion(s32[2048]{0:T(1024)S(1)} %bitcast.114, s32[2048]{0:T(1024)S(1)} %bitcast.116, s32[]{:T(128)} %constant.11.clone.1), kind=kCustom, calls=%fused_computation.107 | custom fusion | bytes 16388
  286.1 10.4 %all-to-all-start = ((s32[4,64,16]{2,0,1:T(4,128)}), s32[4,64,16]{2,0,1:T(4,128)S(1)}, u32[]{:S(2)}, u32[]{:S(2)}) async-start(s32[4,64,16]{2,0,1:T(4,128)} %copy.33), calls=%async_computation | async-start | bytes 262144 | tf_op jit(solution)/shard_map/all_to_all | solution.py:109
  296.5 1.5 fusion.15
  298.0 1.6 copy.35
  299.6 7.9 %all-to-all-done = s32[4,64,16]{2,0,1:T(4,128)S(1)} async-done(((s32[4,64,16]{2,0,1:T(4,128)}), s32[4,64,16]{2,0,1:T(4,128)S(1)}, u32[]{:S(2)}, u32[]{:S(2)}) %all-to-all-start) | async-done | bytes 16416 | tf_op jit(solution)/shard_map/all_to_all | solution.py:109
  307.6 5.6 %all-to-all-start.1 = ((bf16[4,64,16,256]{3,2,0,1:T(8,128)(2,1)}), bf16[4,64,16,256]{3,2,0,1:T(8,128)(2,1)}, u32[]{:S(2)}, u32[]{:S(2)}) async-start(bf16[4,64,16,256]{3,2,0,1:T(8,128)(2,1)} %copy.35), calls=%async_computation.1 | async-start | bytes 4194304 | tf_op jit(solution)/shard_map/all_to_all | solution.py:102
  313.1 2.9 copy.38
  316.2 49.0 %all-to-all-done.1 = bf16[4,64,16,256]{3,2,0,1:T(8,128)(2,1)} async-done(((bf16[4,64,16,256]{3,2,0,1:T(8,128)(2,1)}), bf16[4,64,16,256]{3,2,0,1:T(8,128)(2,1)}, u32[]{:S(2)}, u32[]{:S(2)}) %all-to-all-start.1) | async-done | bytes 2097184 | tf_op jit(solution)/shard_map/all_to_all | solution.py:102
  365.2 1.8 copy.36
  367.0 2.9 multiply_reduce_fusion
  370.5 1.9 divide_subtract_fusion
  372.4 2.9 copy.49
  375.3 1.3 fusion.24
  376.7 54.5 %all-gather.1 = f32[64,3,1024]{2,1,0:T(4,128)} all-gather(f32[1,3,1024]{2,1,0:T(4,128)S(1)} %maximum_bitcast_fusion), channel_id=2, replica_groups=mesh['dp'=64,'mp'=4] {'dp'}, dimensions={0}, use_global_device_ids=true | all-gather | bytes 798720 | tf_op jit(solution)/shard_map/all_gather | solution.py:200
  431.2 2.0 reduce_sum.79
  433.2 2.8 fusion.20
  436.0 1.5 fusion.79
  (101 shorter events, 10.7 us)
Async XLA Ops:
  7.2 289.4 %copy-start = (bf16[4,512,256]{2,1,0:T(8,128)(2,1)S(1)}, bf16[4,512,256]{2,1,0:T(8,128)(2,1)}, u32[]{:S(2)}) copy-start(bf16[4,512,256]{2,1,0:T(8,128)(2,1)} %param.15) | copy-start | bytes 3145732
  7.2 3.1 copy-start.23
  7.2 3.2 copy-start.22
  7.2 3.0 copy-start.15
  7.2 3.4 copy-start.16
  7.2 32.8 %copy-start.9 = (f32[4,512,256]{2,1,0:T(8,128)S(1)}, f32[4,512,256]{2,1,0:T(8,128)}, u32[]{:S(2)}) copy-start(f32[4,512,256]{2,1,0:T(8,128)} %param.13) | copy-start | bytes 6291460
  43.8 56.1 %all-to-all-start.3 = ((bf16[4,64,16,256]{3,2,0,1:T(8,128)(2,1)}), bf16[4,64,16,256]{3,2,0,1:T(8,128)(2,1)S(1)}, u32[]{:S(2)}, u32[]{:S(2)}) async-start(bf16[4,64,16,256]{3,2,0,1:T(8,128)(2,1)} %copy.45), calls=%async_computation.3 | async-start | bytes 4194304 | tf_op jit(solution)/shard_map/all_to_all | solution.py:144
  48.5 2.5 copy-start.20
  48.5 75.4 %reduce-scatter.6.cloned.1.call-start = ((), (), s32[]{:S(2)}) async-start(), calls=%async_computation.9 | async-start | bytes 655360 | tf_op jit(solution)/shard_map/reduce_scatter | solution.py:63
  100.0 2.1 copy-start.12
  102.1 1.4 copy-start.17
  103.4 61.9 %reduce-scatter.8.cloned.1.call-start = ((), (), s32[]{:S(2)}) async-start(), calls=%async_computation.10 | async-start | bytes 655360 | tf_op jit(solution)/shard_map/reduce_scatter | solution.py:63
  123.9 16.2 %copy-start.13 = (bf16[2,512,1024]{2,1,0:T(8,128)(2,1)S(1)}, bf16[2,512,1024]{2,1,0:T(8,128)(2,1)}, u32[]{:S(2)}) copy-start(bf16[2,512,1024]{2,1,0:T(8,128)(2,1)} %param.23) | copy-start | bytes 6291460
  137.3 4.1 copy-start.7
  140.1 41.3 %copy-start.4 = (bf16[256,1024]{1,0:T(8,128)(2,1)}, bf16[256,1024]{1,0:T(8,128)(2,1)S(1)}, u32[]{:S(2)}) copy-start(bf16[256,1024]{1,0:T(8,128)(2,1)S(1)} %get-tuple-element.48) | copy-start | bytes 1572868
  140.1 1.4 copy-start.14
  141.4 75.1 %reduce-scatter.10.cloned.1.call-start = ((), (), s32[]{:S(2)}) async-start(), calls=%async_computation.11 | async-start | bytes 655360 | tf_op jit(solution)/shard_map/reduce_scatter | solution.py:63
  166.2 23.5 %copy-start.21 = (s32[256]{0:T(256)S(1)}, s32[256]{0:T(256)}, u32[]{:S(2)}) copy-start(s32[256]{0:T(256)} %param.21) | copy-start | bytes 3076
  192.7 64.7 %reduce-scatter.12.cloned.1.call-start = ((), (), s32[]{:S(2)}) async-start(), calls=%async_computation.12 | async-start | bytes 655360 | tf_op jit(solution)/shard_map/reduce_scatter | solution.py:63
  216.5 15.7 %copy-start.3 = (bf16[2,512,1024]{2,1,0:T(8,128)(2,1)S(1)}, bf16[2,512,1024]{2,1,0:T(8,128)(2,1)}, u32[]{:S(2)}) copy-start(bf16[2,512,1024]{2,1,0:T(8,128)(2,1)} %param.22) | copy-start | bytes 6291460
  229.8 0.7 copy-start.10
  233.5 202.5 %reduce-scatter.14.cloned.1.call-start = ((), (), s32[]{:S(2)}) async-start(), calls=%async_computation.13 | async-start | bytes 8519680 | tf_op jit(solution)/shard_map/reduce_scatter | solution.py:33
  233.8 1.9 copy-start.5
  233.8 1.9 copy-start.11
  235.7 1.8 copy-start.8
  257.4 13.8 %copy-start.2 = (f32[1,512,1024]{2,1,0:T(8,128)S(1)}, f32[1,512,1024]{2,1,0:T(8,128)}, u32[]{:S(2)}) copy-start(f32[1,512,1024]{2,1,0:T(8,128)} %convolution_bitcast_fusion.2) | copy-start | bytes 6291460
  276.5 0.7 copy-start.18
  286.1 21.5 %all-to-all-start = ((s32[4,64,16]{2,0,1:T(4,128)}), s32[4,64,16]{2,0,1:T(4,128)S(1)}, u32[]{:S(2)}, u32[]{:S(2)}) async-start(s32[4,64,16]{2,0,1:T(4,128)} %copy.33), calls=%async_computation | async-start | bytes 262144 | tf_op jit(solution)/shard_map/all_to_all | solution.py:109
  307.6 57.6 %all-to-all-start.1 = ((bf16[4,64,16,256]{3,2,0,1:T(8,128)(2,1)}), bf16[4,64,16,256]{3,2,0,1:T(8,128)(2,1)}, u32[]{:S(2)}, u32[]{:S(2)}) async-start(bf16[4,64,16,256]{3,2,0,1:T(8,128)(2,1)} %copy.35), calls=%async_computation.1 | async-start | bytes 4194304 | tf_op jit(solution)/shard_map/all_to_all | solution.py:102
  367.0 2.9 copy-start.19
  367.0 3.5 copy-start.1
  375.3 57.9 %copy-start.6 = (f32[256,1024]{1,0:T(8,128)S(1)}, f32[256,1024]{1,0:T(8,128)}, u32[]{:S(2)}) copy-start(f32[256,1024]{1,0:T(8,128)} %get-tuple-element.50) | copy-start | bytes 3145732
Sparse Core Ops, SparseCore 0:
  103.5 20.3 reduce-scatter.5
  141.5 23.7 reduce-scatter.7
  192.8 23.5 reduce-scatter.9
  233.7 23.7 reduce-scatter.11
  276.6 151.3 reduce-scatter.13
